TPU v7x, 32 devices: a whole 2x2x4 slice. The times are simulated.
32 devices in a mesh: parts: 2 (over y), filt: 4 (over z), space: 4 (over x, core).
Axes of the slice: x: 2, y: 2, z: 4, core: 2. Of those that a mesh axis runs over, the one named last changes fastest.
Arguments:
- volume: bfloat16 [512, 16, 8, 128], P('filt', ('parts', 'space')), parts along dimension 1, may hold values from -6 to 6
- weight: bfloat16 [512, 27, 512], P('filt'), may hold values from -0.0546875 to 0.0546875
- bias: float32 [512], P('filt'), may hold values from -3 to 3
- upstream: bfloat16 [512, 16, 8, 128], P('filt', ('parts', 'space')), parts along dimension 1, may hold values from -0.0625 to 0.0625
Outputs:
- features: bfloat16 [512, 16, 8, 128], P('filt', ('parts', 'space')), parts along dimension 1
- weight_grad: float32 [1024, 27, 512], P(('parts', 'filt')), parts along dimension 0
There are 2 independent parts, one for each index of `parts`. A program takes and returns all parts, laid end to end along the dimension named above; an argument that names none is the same for every part. Nothing has to cross between parts.
All inputs are finite; a program needn't handle non-finite values.
Results may differ from a plain program's by a relative error of at most 0.001.
Values may be sent and summed in bfloat16 or wider, within the bound.
No kernel may reach another device: no remote copies, remote signals or barrier semaphores. Data moves between devices by JAX's collectives and lax.ppermute only.
A program may use at most 128 MiB of HBM per device.

v0:
```python
import jax
import jax.numpy as jnp
from jax import lax
from jax.sharding import PartitionSpec as P


def padded(block, sides, width):
    for axis, dim in sides:
        count = lax.axis_size(axis)
        forward = [(i, i + 1) for i in range(count - 1)]
        backward = [(target, source) for source, target in forward]
        low = lax.ppermute(
            lax.slice_in_dim(block, block.shape[dim] - width, None, axis=dim), axis, forward
        )
        high = lax.ppermute(lax.slice_in_dim(block, 0, width, axis=dim), axis, backward)
        block = jnp.concatenate([low, block, high], axis=dim)
    return block


def convolve(slab, kernel):
    return lax.conv_general_dilated(
        slab[None],
        kernel,
        (1, 1, 1),
        [(0, 0), (1, 1), (1, 1)],
        dimension_numbers=("NCDHW", "OIDHW", "NCDHW"),
        preferred_element_type=jnp.float32,
    )[0]


def shifted_slopes(upstream):
    out_dev = upstream.shape[0]
    depth = upstream.shape[1]
    height = upstream.shape[2]
    length = upstream.shape[3]
    spread = jnp.pad(upstream, ((0, 0), (2, 2), (1, 1), (1, 1)))
    copies = []
    for tap in range(27):
        first = tap // 9
        second = tap // 3 % 3
        third = tap % 3
        copies.append(
            spread[
                :,
                2 - first : 4 - first + depth,
                2 - second : 2 - second + height,
                2 - third : 2 - third + length,
            ]
        )
    stacked = jnp.stack(copies, 1)
    return stacked.reshape(out_dev * 27, (depth + 2) * height * length)


def tap_grads(slab, slopes, out_dev):
    flat = slab.reshape(slab.shape[0], -1)
    product = lax.dot_general(
        slopes, flat, (((1,), (1,)), ((), ())), preferred_element_type=jnp.float32
    )
    return product.reshape(out_dev, 27, slab.shape[0])


def on_device(volume, weight, bias, upstream):
    out_dev = weight.shape[0]
    in_all = weight.shape[2]
    kernel = weight.reshape(out_dev, 3, 3, 3, in_all).transpose(0, 4, 1, 2, 3)
    slopes = shifted_slopes(upstream)
    whole = lax.all_gather(volume, "filt", axis=0, tiled=True)
    rimmed = padded(whole, (("space", 1),), 1)
    pre = convolve(rimmed, kernel)
    partial_grads = tap_grads(rimmed, slopes, out_dev)
    weight_grad = lax.psum(partial_grads, "space")
    pre = pre + bias[:, None, None, None]
    features = jnp.where(pre > 0, pre, 0.3 * pre).astype(jnp.bfloat16)
    return (features, weight_grad)


def solution(mesh):
    return jax.shard_map(
        on_device,
        mesh=mesh,
        in_specs=(
            P("filt", ("parts", "space"), None, None),
            P("filt", None, None),
            P("filt"),
            P("filt", ("parts", "space"), None, None),
        ),
        out_specs=(P("filt", ("parts", "space"), None, None), P(("parts", "filt"), None, None)),
        check_vma=False,
    )
```

profile of v0, /device:TPU:0, one launch (start us, length us, event | category | flops | bytes accessed | tf_op | source)
XLA Modules:
  0.0 254.6 jit_solution(8644923369791404062)
XLA Ops:
  7.2 2.1 copy.8
  9.4 1.2 copy.13
  10.6 1.3 fusion.19
  11.9 1.2 fusion.21
  13.1 1.3 fusion.23
  14.3 1.3 fusion.25
  15.6 1.1 fusion.27
  16.8 1.3 fusion.29
  18.1 1.3 fusion.31
  19.4 1.2 fusion.33
  20.5 1.4 fusion.35
  21.9 1.2 fusion.37
  23.1 1.1 fusion.39
  24.3 1.3 fusion.41
  25.6 1.4 fusion.43
  26.9 1.1 fusion.45
  28.1 1.3 fusion.47
  29.4 1.3 fusion.49
  30.6 1.1 fusion.51
  31.8 1.3 fusion.53
  33.1 1.3 fusion.55
  34.4 24.5 %all-gather.2.cloned.1.call-done = bf16[512,2,8,128]{3,0,2,1:T(8,128)(2,1)} async-done(((bf16[128,2,8,128]{3,0,2,1:T(8,128)(2,1)}), bf16[512,2,8,128]{3,0,2,1:T(8,128)(2,1)}) %all-gather.2.cloned.1.call-update) | async-done | bytes 2097168 | tf_op jit(solution)/shard_map/all_gather | solution.py:67
  58.8 1.7 fusion.76
  60.5 1.8 collective-permute-start
  62.3 2.2 fusion.57
  64.5 2.3 fusion.59
  66.8 1.3 collective-permute-start.1
  68.1 2.3 fusion.61
  70.4 2.2 fusion.63
  72.6 2.3 fusion.65
  75.0 2.4 fusion.67
  77.3 2.1 fusion.69
  79.5 2.3 fusion.71
  81.8 0.1 constant_dynamic-update-slice_fusion.2
  81.9 1.9 constant_dynamic-update-slice_fusion.1
  83.8 0.1 constant_dynamic-update-slice_fusion
  84.0 2.0 copy-done.2
  86.0 20.7 %fusion.10 = f32[128,27,512]{2,0,1:T(8,128)} fusion(bf16[128,27,4,8,128]{4,0,3,2,1:T(8,128)(2,1)} %fusion.71, bf16[512,4,8,128]{3,0,2,1:T(8,128)(2,1)S(1)} %constant_dynamic-update-slice_fusion), kind=kOutput, calls=%fused_computation.38 | convolution fusion | flops 14495514624 | bytes 39583744 | tf_op jit(solution)/shard_map/dot_general | solution.py:56
  106.7 8.0 %copy.18 = bf16[512,4,8,1,128]{0,2,4,1,3:T(8,128)(2,1)} copy(bf16[512,4,8,1,128]{4,0,2,1,3:T(8,128)(2,1)} %bitcast.144) | data formatting | bytes 8388608
  114.7 2.6 %pad.5.clone = bf16[512,4,8,1,136]{0,2,4,1,3:T(8,128)(2,1)S(1)} pad(bf16[512,4,8,1,128]{0,2,4,1,3:T(8,128)(2,1)} %copy.18, bf16[]{:T(256)} %constant.6.clone.1), padding=0_0x0_0x0_0x0_0x1_7 | pad | bytes 8650754 | tf_op jit(solution)/shard_map/broadcast_in_dim | solution.py:22
  117.3 1.7 copy.11
  119.1 0.1 slice.120
  119.2 16.9 %fusion.14 = f32[2,8,8,17,128]{4,2,3,1,0:T(8,128)S(1)} fusion(bf16[128,3,3,3,512]{4,0,3,2,1:T(8,128)(2,1)S(1)} %bitcast.142, bf16[512,4,8,1,7,2]{0,4,5,2,1,3:T(8,128)(2,1)S(1)} %slice.120, bf16[512,4,8,1,8,17]{0,4,5,2,1,3:T(8,128)(2,1)S(1)} %copy.11, pred[8,17]{0,1:T(8,128)(4,1)S(1)} %copy-done.4), kind=kOutput, calls=%fused_computation.40 | convolution fusion | flops 7074234368 | bytes 9568392 | tf_op jit(solution)/shard_map/conv_general_dilated | solution.py:21
  136.1 0.2 copy.12
  136.3 1.0 fusion.17
  137.3 2.4 copy.14
  139.7 100.7 %all-reduce.3.cloned.1.call-done = f32[128,27,512]{2,0,1:T(8,128)} async-done(((f32[128,27,512]{2,0,1:T(8,128)}), f32[128,27,512]{2,0,1:T(8,128)}) %all-reduce.3.cloned.1.call-update) | async-done | bytes 7077904 | tf_op jit(solution)/shard_map/psum | solution.py:71
  240.4 7.3 %copy.48 = f32[128,27,512]{2,0,1:T(8,128)} copy(f32[128,27,512]{2,0,1:T(8,128)} %all-reduce.3.cloned.1.call-done) | data formatting | bytes 14155776
  (15 shorter events, 0.1 us)
Async XLA Ops:
  7.2 112.0 %copy-start = (bf16[128,27,512]{2,0,1:T(8,128)(2,1)S(1)}, bf16[128,27,512]{2,0,1:T(8,128)(2,1)}, u32[]{:S(2)}) copy-start(bf16[128,27,512]{2,0,1:T(8,128)(2,1)} %param.5) | copy-start | bytes 10616836
  7.2 51.7 %all-gather.2.cloned.1.call-start = ((), (), s32[]{:S(2)}) async-start(), calls=%async_computation | async-start | bytes 2621440 | tf_op jit(solution)/shard_map/all_gather | solution.py:67
  9.4 231.0 %all-reduce.3.cloned.1.call-start = ((), (), s32[]{:S(2)}) async-start(), calls=%async_computation.1 | async-start | bytes 14155776 | tf_op jit(solution)/shard_map/psum | solution.py:71
  10.6 22.5 %copy-start.1 = (bf16[128,2,8,128]{3,0,2,1:T(8,128)(2,1)}, bf16[128,2,8,128]{3,0,2,1:T(8,128)(2,1)S(1)}, u32[]{:S(2)}) copy-start(bf16[128,2,8,128]{3,0,2,1:T(8,128)(2,1)S(1)} %copy.13) | copy-start | bytes 1572868
  60.5 21.2 %collective-permute-start = (bf16[512,1,8,128]{3,0,2,1:T(8,128)(2,1)S(1)}, bf16[512,1,8,128]{3,0,2,1:T(8,128)(2,1)S(1)}, u32[]{:S(2)}, u32[]{:S(2)}) collective-permute-start(bf16[512,1,8,128]{3,0,2,1:T(8,128)(2,1)S(1)} %get-tuple-element.5), channel_id=1, source_target_pairs={{0,1},{1,2},{2,3},{4,5},{5,6},{6,7},{8,9},{9,10},{10,11},{12,13},{... | collective-permute-start | bytes 3145736 | tf_op jit(solution)/shard_map/ppermute | solution.py:12
  66.8 17.0 %collective-permute-start.1 = (bf16[512,1,8,128]{3,0,2,1:T(8,128)(2,1)S(1)}, bf16[512,1,8,128]{3,0,2,1:T(8,128)(2,1)S(1)}, u32[]{:S(2)}, u32[]{:S(2)}) collective-permute-start(bf16[512,1,8,128]{3,0,2,1:T(8,128)(2,1)S(1)} %get-tuple-element.4), channel_id=1, source_target_pairs={{1,0},{2,1},{3,2},{5,4},{6,5},{7,6},{9,8},{10,9},{11,10},{13,12},{... | collective-permute-start | bytes 3145736 | tf_op jit(solution)/shard_map/ppermute | solution.py:15
  83.9 2.0 copy-start.2
  106.6 12.6 %copy-start.4 = (pred[8,17]{0,1:T(8,128)(4,1)S(1)}, pred[8,17]{0,1:T(8,128)(4,1)}, u32[]{:S(2)}) copy-start(pred[8,17]{0,1:T(8,128)(4,1)} %constant.15) | copy-start | bytes 412
  119.2 17.1 %copy-start.3 = (f32[128]{0:T(128)S(1)}, f32[128]{0:T(128)}, u32[]{:S(2)}) copy-start(f32[128]{0:T(128)} %param.6) | copy-start | bytes 1540
Sparse Core Ops, SparseCore 0:
  10.2 48.6 all-gather.1
  106.8 133.5 all-reduce.2
where the time goes:
time: 255 us
  waiting for transfers between devices  125 us (49%)
  local copies, waits for them, and re-layouts  73.5 us (29%)
  matrix products  37.5 us (15%)
  between operations  14.2 us (6%)
  starting transfers between devices  3.13 us (1%)
    psum x1, waiting for transfers between devices, on_device(): weight_grad = lax.psum(partial_grads, 'space')  101 us
    unnamed x43, local copies, waits for them, and re-layouts  64.7 us
    all_gather x1, waiting for transfers between devices, on_device(): whole = lax.all_gather(volume, 'filt', axis=0, tiled=True)  24.5 us
    dot_general x1, matrix products, tap_grads(): lax.dot_general(slopes, flat, (((1,), (1,)), ((), ())), preferred_element...  20.7 us
    conv_general_dilated x1, matrix products, convolve(): lax.conv_general_dilated(slab[None], kernel, (1, 1, 1), [(0, 0), (1, 1),...  16.9 us
  transfers between devices with their start and end apart: 4, of which 2 were waited for; matrix products, arithmetic and copies ran while one was open for 31% of the time, Pallas kernels for 0%

commit v1 on v0

--- a/solution.py
+++ b/solution.py
@@ -2,6 +2,11 @@
 import jax.numpy as jnp
 from jax import lax
 from jax.sharding import PartitionSpec as P
+
+
+def gather_and_add(array, axis):
+    pieces = lax.all_gather(array, axis)
+    return jnp.sum(pieces, axis=0)
 
 
 def padded(block, sides, width):
@@ -68,7 +73,7 @@
     rimmed = padded(whole, (("space", 1),), 1)
     pre = convolve(rimmed, kernel)
     partial_grads = tap_grads(rimmed, slopes, out_dev)
-    weight_grad = lax.psum(partial_grads, "space")
+    weight_grad = gather_and_add(partial_grads, "space")
     pre = pre + bias[:, None, None, None]
     features = jnp.where(pre > 0, pre, 0.3 * pre).astype(jnp.bfloat16)
     return (features, weight_grad)

time: 255 us -> 303 us (1.19)
  waiting for transfers between devices: 125 us -> 164 us
  other arithmetic: 0.96 us -> 15.7 us
  local copies, waits for them, and re-layouts: 73.5 us -> 67 us
    all_gather x0 -> x1, waiting for transfers between devices: none -> 140 us  [gather_and_add(): pieces = lax.all_gather(array, axis)]
    psum x1 -> x0, waiting for transfers between devices: 101 us -> none  [on_device(): weight_grad = lax.psum(partial_grads, 'space')]
    reduce_sum x0 -> x1, other arithmetic: none -> 14.8 us  [gather_and_add(): return jnp.sum(pieces, axis=0)]
    unnamed x43 -> x42, local copies, waits for them, and re-layouts: 64.7 us -> 57.3 us
  transfers between devices with their start and end apart: 4 -> 4, of which waited for: 2 -> 2; matrix products, arithmetic and copies ran while one was open for 31% -> 26% of each run, Pallas kernels for 0% -> 0%
where the time goes in v1:
time: 303 us; the launch traced here: 302 us
  waiting for transfers between devices  164 us (54%)
  local copies, waits for them, and re-layouts  67 us (22%)
  matrix products  37.5 us (12%)
  other arithmetic  15.7 us (5%)
  between operations  14.2 us (5%)
  starting transfers between devices  3.13 us (1%)
    all_gather x1, waiting for transfers between devices, gather_and_add(): pieces = lax.all_gather(array, axis)  140 us
    unnamed x42, local copies, waits for them, and re-layouts  57.3 us
    all_gather x1, waiting for transfers between devices, on_device(): whole = lax.all_gather(volume, 'filt', axis=0, tiled=True)  24.5 us
    dot_general x1, matrix products, tap_grads(): lax.dot_general(slopes, flat, (((1,), (1,)), ((), ())), preferred_element...  20.7 us
    conv_general_dilated x1, matrix products, convolve(): lax.conv_general_dilated(slab[None], kernel, (1, 1, 1), [(0, 0), (1, 1),...  16.9 us
    reduce_sum x1, other arithmetic, gather_and_add(): return jnp.sum(pieces, axis=0)  14.8 us
  transfers between devices with their start and end apart: 4, of which 2 were waited for; matrix products, arithmetic and copies ran while one was open for 26% of the time, Pallas kernels for 0%

profile of v1, /device:TPU:0, one launch (start us, length us, event | category | flops | bytes accessed | tf_op | source)
XLA Modules:
  0.0 301.8 jit_solution(11401252176695299645)
XLA Ops:
  7.2 2.1 copy.8
  9.4 1.2 copy.13
  10.6 1.3 fusion.19
  11.9 1.2 fusion.21
  13.1 1.3 fusion.23
  14.3 1.3 fusion.25
  15.6 1.1 fusion.27
  16.8 1.3 fusion.29
  18.1 1.3 fusion.31
  19.4 1.2 fusion.33
  20.5 1.4 fusion.35
  21.9 1.2 fusion.37
  23.1 1.1 fusion.39
  24.3 1.3 fusion.41
  25.6 1.4 fusion.43
  26.9 1.1 fusion.45
  28.1 1.3 fusion.47
  29.4 1.3 fusion.49
  30.6 1.1 fusion.51
  31.8 1.3 fusion.53
  33.1 1.3 fusion.55
  34.4 24.5 %all-gather.4.cloned.1.call-done = bf16[512,2,8,128]{3,0,2,1:T(8,128)(2,1)} async-done(((bf16[128,2,8,128]{3,0,2,1:T(8,128)(2,1)}), bf16[512,2,8,128]{3,0,2,1:T(8,128)(2,1)}) %all-gather.4.cloned.1.call-update) | async-done | bytes 2097168 | tf_op jit(solution)/shard_map/all_gather | solution.py:72
  58.8 1.7 fusion.76
  60.5 1.8 collective-permute-start
  62.3 2.2 fusion.57
  64.5 2.3 fusion.59
  66.8 1.3 collective-permute-start.1
  68.1 2.3 fusion.61
  70.4 2.2 fusion.63
  72.6 2.3 fusion.65
  75.0 2.4 fusion.67
  77.3 2.1 fusion.69
  79.5 2.3 fusion.71
  81.8 0.1 constant_dynamic-update-slice_fusion.2
  81.9 1.9 constant_dynamic-update-slice_fusion.1
  83.8 0.1 constant_dynamic-update-slice_fusion
  84.0 2.0 copy-done.2
  86.0 20.7 %fusion.10 = f32[128,27,512]{2,0,1:T(8,128)} fusion(bf16[128,27,4,8,128]{4,0,3,2,1:T(8,128)(2,1)} %fusion.71, bf16[512,4,8,128]{3,0,2,1:T(8,128)(2,1)S(1)} %constant_dynamic-update-slice_fusion), kind=kOutput, calls=%fused_computation.38 | convolution fusion | flops 14495514624 | bytes 39583744 | tf_op jit(solution)/shard_map/dot_general | solution.py:61
  106.7 8.0 %copy.18 = bf16[512,4,8,1,128]{0,2,4,1,3:T(8,128)(2,1)} copy(bf16[512,4,8,1,128]{4,0,2,1,3:T(8,128)(2,1)} %bitcast.146) | data formatting | bytes 8388608
  114.6 3.6 %pad.5.clone = bf16[512,4,8,1,136]{0,2,4,1,3:T(8,128)(2,1)S(1)} pad(bf16[512,4,8,1,128]{0,2,4,1,3:T(8,128)(2,1)} %copy.18, bf16[]{:T(256)} %constant.2.clone.1), padding=0_0x0_0x0_0x0_0x1_7 | pad | bytes 8650754 | tf_op jit(solution)/shard_map/broadcast_in_dim | solution.py:27
  118.2 1.7 copy.11
  119.9 0.1 slice.120
  120.1 16.9 %fusion.14 = f32[2,8,8,17,128]{4,2,3,1,0:T(8,128)S(1)} fusion(bf16[128,3,3,3,512]{4,0,3,2,1:T(8,128)(2,1)S(1)} %bitcast.143, bf16[512,4,8,1,7,2]{0,4,5,2,1,3:T(8,128)(2,1)S(1)} %slice.120, bf16[512,4,8,1,8,17]{0,4,5,2,1,3:T(8,128)(2,1)S(1)} %copy.11, pred[8,17]{0,1:T(8,128)(4,1)S(1)} %copy-done.4), kind=kOutput, calls=%fused_computation.40 | convolution fusion | flops 7074234368 | bytes 9568392 | tf_op jit(solution)/shard_map/conv_general_dilated | solution.py:26
  137.0 0.2 copy.12
  137.2 1.0 fusion.17
  138.2 2.4 copy.14
  140.6 139.7 %all-gather.6.cloned.1.call-done = f32[512,27,512]{2,0,1:T(8,128)} async-done(((f32[128,27,512]{2,0,1:T(8,128)}), f32[512,27,512]{2,0,1:T(8,128)}) %all-gather.6.cloned.1.call-update) | async-done | bytes 28311568 | tf_op jit(solution)/shard_map/all_gather | solution.py:8
  280.2 14.8 %reduce_sum.9 = f32[128,27,512]{2,0,1:T(8,128)} reduce(f32[4,128,27,512]{3,1,0,2:T(8,128)} %bitcast.144, f32[]{:T(128)} %constant.3.clone.1), dimensions={0}, to_apply=%region_0.1 | reduce | flops 5308416 | bytes 35389444 | tf_op jit(solution)/shard_map/reduce_sum | solution.py:9
  (15 shorter events, 0.1 us)
Async XLA Ops:
  7.2 112.9 %copy-start = (bf16[128,27,512]{2,0,1:T(8,128)(2,1)S(1)}, bf16[128,27,512]{2,0,1:T(8,128)(2,1)}, u32[]{:S(2)}) copy-start(bf16[128,27,512]{2,0,1:T(8,128)(2,1)} %param.5) | copy-start | bytes 10616836
  7.2 51.7 %all-gather.4.cloned.1.call-start = ((), (), s32[]{:S(2)}) async-start(), calls=%async_computation | async-start | bytes 2621440 | tf_op jit(solution)/shard_map/all_gather | solution.py:72
  9.4 270.9 %all-gather.6.cloned.1.call-start = ((), (), s32[]{:S(2)}) async-start(), calls=%async_computation.1 | async-start | bytes 35389440 | tf_op jit(solution)/shard_map/all_gather | solution.py:8
  10.6 22.5 %copy-start.1 = (bf16[128,2,8,128]{3,0,2,1:T(8,128)(2,1)}, bf16[128,2,8,128]{3,0,2,1:T(8,128)(2,1)S(1)}, u32[]{:S(2)}) copy-start(bf16[128,2,8,128]{3,0,2,1:T(8,128)(2,1)S(1)} %copy.13) | copy-start | bytes 1572868
  60.5 21.2 %collective-permute-start = (bf16[512,1,8,128]{3,0,2,1:T(8,128)(2,1)S(1)}, bf16[512,1,8,128]{3,0,2,1:T(8,128)(2,1)S(1)}, u32[]{:S(2)}, u32[]{:S(2)}) collective-permute-start(bf16[512,1,8,128]{3,0,2,1:T(8,128)(2,1)S(1)} %get-tuple-element.5), channel_id=1, source_target_pairs={{0,1},{1,2},{2,3},{4,5},{5,6},{6,7},{8,9},{9,10},{10,11},{12,13},{... | collective-permute-start | bytes 3145736 | tf_op jit(solution)/shard_map/ppermute | solution.py:17
  66.8 17.0 %collective-permute-start.1 = (bf16[512,1,8,128]{3,0,2,1:T(8,128)(2,1)S(1)}, bf16[512,1,8,128]{3,0,2,1:T(8,128)(2,1)S(1)}, u32[]{:S(2)}, u32[]{:S(2)}) collective-permute-start(bf16[512,1,8,128]{3,0,2,1:T(8,128)(2,1)S(1)} %get-tuple-element.4), channel_id=1, source_target_pairs={{1,0},{2,1},{3,2},{5,4},{6,5},{7,6},{9,8},{10,9},{11,10},{13,12},{... | collective-permute-start | bytes 3145736 | tf_op jit(solution)/shard_map/ppermute | solution.py:20
  83.9 2.0 copy-start.2
  106.6 13.4 %copy-start.4 = (pred[8,17]{0,1:T(8,128)(4,1)S(1)}, pred[8,17]{0,1:T(8,128)(4,1)}, u32[]{:S(2)}) copy-start(pred[8,17]{0,1:T(8,128)(4,1)} %constant.16) | copy-start | bytes 412
  120.1 17.1 %copy-start.3 = (f32[128]{0:T(128)S(1)}, f32[128]{0:T(128)}, u32[]{:S(2)}) copy-start(f32[128]{0:T(128)} %param.6) | copy-start | bytes 1540
Sparse Core Ops, SparseCore 0:
  10.2 48.6 all-gather.3
  106.8 173.4 all-gather.5
